TPU v7x, 512 devices: a whole 4x8x8 slice. The times are simulated.
512 devices in a mesh: ctx: 32 (over z, x), exp: 16 (over y, core).
Axes of the slice: x: 4, y: 8, z: 8, core: 2. Of those that a mesh axis runs over, the one named last changes fastest.
Arguments:
- stream: bfloat16 [16, 4096, 1024], P('exp', 'ctx'), may hold values from -400 to 400
- queries: bfloat16 [16, 4096, 16, 128], P('exp', 'ctx'), may hold values from -6 to 6
- key_rows: bfloat16 [16, 4096, 2, 128], P('exp', 'ctx'), may hold values from -4 to 4
- value_rows: bfloat16 [16, 4096, 2, 128], P('exp', 'ctx'), may hold values from -6 to 6
- expert_ids: int32 [16, 4096, 2], P('exp', 'ctx'), may hold values from 0 to 127, as said below
- norm_gain: bfloat16 [1024], replicated, may hold values from 0.099609375 to 1.8984375
- router_weight: bfloat16 [1024, 128], replicated, may hold values from -0.1875 to 0.1875
- gate_weight: bfloat16 [98304, 1024], P(('ctx', 'exp')), may hold values from -0.1875 to 0.1875
- up_weight: bfloat16 [98304, 1024], P(('ctx', 'exp')), may hold values from -0.1875 to 0.1875
- down_weight: bfloat16 [98304, 1024], P(('ctx', 'exp')), may hold values from -0.21875 to 0.21875
Outputs:
- attended: bfloat16 [16, 4096, 16, 128], P('exp', 'ctx')
- expert_mix: bfloat16 [16, 4096, 1024], P('exp', 'ctx')
Inputs may be any that keep to these rules, and one draw needn't show every extreme that they name: `expert_ids`: within the rows of one device (aligned blocks of 128 positions of one sequence), a token's 2 experts differ and no expert is named more than 4 times; one expert is named exactly 4 times in every such block.
All inputs are finite; a program needn't handle non-finite values.
Results may differ from a plain program's by a relative error of at most 0.01.
Values may be sent and summed in bfloat16 or wider, within the bound.
No kernel may reach another device: no remote copies, remote signals or barrier semaphores. Data moves between devices by JAX's collectives and lax.ppermute only.
A program may use at most 64 MiB of HBM per device.

v0:
```python
import math
import jax
import jax.numpy as jnp
from jax import lax
from jax.sharding import PartitionSpec as P


def from_partner(value, axis, bit):
    return lax.ppermute(value, axis, [(i, i ^ 1 << bit) for i in range(lax.axis_size(axis))])


def expert_rows(inputs, gate_rows, up_rows, down_rows):
    features = inputs.shape[-1]
    flat_rows = inputs.reshape(-1, features)
    contract = (((1,), (1,)), ((), ()))
    gate_part = lax.dot_general(flat_rows, gate_rows, contract, preferred_element_type=jnp.float32)
    up_part = lax.dot_general(flat_rows, up_rows, contract, preferred_element_type=jnp.float32)
    hidden = (jax.nn.silu(gate_part) * up_part).astype(jnp.bfloat16)
    projected = jnp.dot(hidden, down_rows, preferred_element_type=jnp.float32)
    return projected.reshape(inputs.shape)


def attention(queries, key_rows, value_rows):
    seq_rows = queries.shape[1]
    head_count = queries.shape[2]
    head_size = queries.shape[3]
    kv_count = key_rows.shape[2]
    group_size = head_count // kv_count
    grouped = queries[0].reshape(seq_rows, kv_count, group_size, head_size)
    scaling = 1.0 / math.sqrt(head_size)
    query_pos = lax.axis_index("ctx") * seq_rows + jnp.arange(seq_rows, dtype=jnp.int32)
    initial = (
        jnp.full((kv_count, group_size, seq_rows), -1e30, jnp.float32),
        jnp.zeros((kv_count, group_size, seq_rows), jnp.float32),
        jnp.zeros((kv_count, group_size, seq_rows, head_size), jnp.float32),
    )
    key_piece = lax.all_gather(key_rows, "ctx", axis=1, tiled=True)
    value_piece = lax.all_gather(value_rows, "ctx", axis=1, tiled=True)
    piece_rows = key_piece.shape[1]
    block_rows = math.gcd(piece_rows, 512)
    block_count = piece_rows // block_rows
    key_blocks = key_piece[0].reshape(block_count, block_rows, kv_count, head_size)
    value_blocks = value_piece[0].reshape(block_count, block_rows, kv_count, head_size)

    def advance(status, members):
        running, totals, accumulated = status
        key_block, value_block, offset = members
        scores = (
            jnp.einsum("qhgd,khd->hgqk", grouped, key_block, preferred_element_type=jnp.float32)
            * scaling
        )
        key_pos = offset * block_rows + jnp.arange(block_rows, dtype=jnp.int32)
        visible = key_pos[None, :] <= query_pos[:, None]
        scores = jnp.where(visible, scores, -1e30)
        highest = jnp.maximum(running, jnp.max(scores, axis=-1))
        factor = jnp.exp(running - highest)
        weights = jnp.where(visible, jnp.exp(scores - highest[..., None]), 0.0)
        totals = totals * factor + jnp.sum(weights, axis=-1)
        accumulated = accumulated * factor[..., None] + jnp.einsum(
            "hgqk,khd->hgqd",
            weights.astype(jnp.bfloat16),
            value_block,
            preferred_element_type=jnp.float32,
        )
        return ((highest, totals, accumulated), None)

    status, unused = lax.scan(
        advance, initial, (key_blocks, value_blocks, jnp.arange(block_count, dtype=jnp.int32))
    )
    running, totals, accumulated = status
    result = accumulated / totals[..., None]
    return (
        jnp.transpose(result, (2, 0, 1, 3))
        .reshape(1, seq_rows, head_count, head_size)
        .astype(jnp.bfloat16)
    )


def local(
    stream,
    queries,
    key_rows,
    value_rows,
    expert_ids,
    norm_gain,
    router_weight,
    gate_weight,
    up_weight,
    down_weight,
):
    attended = attention(queries, key_rows, value_rows)
    ctx_count = lax.axis_size("ctx")
    exp_count = lax.axis_size("exp")
    tokens = stream.shape[1]
    features = stream.shape[2]
    top_count = expert_ids.shape[2]
    expert_total = router_weight.shape[1]
    per_ctx = expert_total // ctx_count
    quarters = exp_count // per_ctx
    capacity = 2 * tokens * top_count // expert_total
    widened = stream[0].astype(jnp.float32)
    mean_square = jnp.mean(widened * widened, axis=-1, keepdims=True)
    normed = (widened * lax.rsqrt(mean_square + 1e-06) * norm_gain.astype(jnp.float32)).astype(
        jnp.bfloat16
    )
    logits = jnp.dot(normed, router_weight, preferred_element_type=jnp.float32)
    chosen = expert_ids[0]
    gate_values = jax.nn.sigmoid(jnp.take_along_axis(logits, chosen, axis=1))
    flat_ids = chosen.reshape(-1)
    onehot = (flat_ids[:, None] == jnp.arange(expert_total, dtype=jnp.int32)[None, :]).astype(
        jnp.int32
    )
    earlier = jnp.cumsum(onehot, axis=0) - onehot
    slot_index = jnp.sum(earlier * onehot, axis=1)
    target = (flat_ids % per_ctx * ctx_count + flat_ids // per_ctx) * capacity + slot_index
    source_rows = jnp.repeat(normed, top_count, axis=0)
    outgoing = (
        jnp.zeros((expert_total * capacity, features), jnp.bfloat16).at[target].set(source_rows)
    )
    outgoing = outgoing.reshape(per_ctx, ctx_count, capacity, features)
    arrived = lax.all_to_all(outgoing, "ctx", split_axis=1, concat_axis=1, tiled=True)
    stacked = jnp.stack([gate_weight, up_weight, down_weight], axis=0)
    my_exp = lax.axis_index("exp")
    partner = from_partner(stacked, "exp", 0)
    upper_side = my_exp & 1 == 1
    held = jnp.where(
        upper_side,
        jnp.concatenate([partner, stacked], axis=1),
        jnp.concatenate([stacked, partner], axis=1),
    )
    half_ctx = ctx_count // 2
    halves_rows = arrived.reshape(per_ctx, 1, 2, half_ctx, capacity, features)
    spread_rows = jnp.broadcast_to(
        halves_rows, (per_ctx, quarters // 2, 2, half_ctx, capacity, features)
    )
    spread_rows = spread_rows.reshape(exp_count, half_ctx, capacity, features)
    received = lax.all_to_all(spread_rows, "exp", split_axis=0, concat_axis=0, tiled=True)
    partials = expert_rows(received, held[0], held[1], held[2])
    returned = lax.all_to_all(
        partials.astype(jnp.bfloat16), "exp", split_axis=0, concat_axis=0, tiled=True
    ).astype(partials.dtype)
    summed = jnp.sum(
        returned.reshape(per_ctx, quarters // 2, 2, half_ctx, capacity, features), axis=1
    )
    finished = summed.astype(jnp.bfloat16).reshape(per_ctx, ctx_count, capacity, features)
    came_back = lax.all_to_all(finished, "ctx", split_axis=1, concat_axis=1, tiled=True)
    flat_back = came_back.reshape(expert_total * capacity, features)
    picked = (
        jnp.take(flat_back, target, axis=0).astype(jnp.float32).reshape(tokens, top_count, features)
    )
    mixture = jnp.sum(picked * gate_values[:, :, None], axis=1).astype(jnp.bfloat16)
    return (attended, mixture[None])


def solution(mesh):
    placed = (
        P("exp", "ctx", None),
        P("exp", "ctx", None, None),
        P("exp", "ctx", None, None),
        P("exp", "ctx", None, None),
        P("exp", "ctx", None),
        P(),
        P(),
        P(("ctx", "exp"), None),
        P(("ctx", "exp"), None),
        P(("ctx", "exp"), None),
    )
    return jax.shard_map(
        local,
        mesh=mesh,
        in_specs=placed,
        out_specs=(P("exp", "ctx", None, None), P("exp", "ctx", None)),
        check_vma=False,
    )
```

profile of v0, /device:TPU:16, one launch (start us, length us, event | category | flops | bytes accessed | tf_op | source)
XLA Modules:
  0.0 309.8 jit_solution(2212090198150793443)
XLA Ops:
  16.4 13.2 %all-to-all-start = ((bf16[4,32,4,1024]{3,2,0,1:T(4,128)(2,1)}), bf16[4,32,4,1024]{3,2,0,1:T(4,128)(2,1)S(1)}, u32[]{:S(2)}, u32[]{:S(2)}) async-start(bf16[4,32,4,1024]{3,2,0,1:T(4,128)(2,1)} %copy.84), calls=%async_computation | async-start | bytes 2097152 | tf_op jit(solution)/shard_map/all_to_all | solution.py:121
  30.3 27.4 %all-to-all-done = bf16[4,32,4,1024]{3,2,0,1:T(4,128)(2,1)S(1)} async-done(((bf16[4,32,4,1024]{3,2,0,1:T(4,128)(2,1)}), bf16[4,32,4,1024]{3,2,0,1:T(4,128)(2,1)S(1)}, u32[]{:S(2)}, u32[]{:S(2)}) %all-to-all-start) | async-done | bytes 1048608 | tf_op jit(solution)/shard_map/all_to_all | solution.py:121
  60.2 7.6 %all-to-all-start.1 = ((bf16[16,16,4,1024]{3,2,1,0:T(4,128)(2,1)}), bf16[16,16,4,1024]{3,2,1,0:T(4,128)(2,1)S(1)}, u32[]{:S(2)}, u32[]{:S(2)}) async-start(bf16[16,16,4,1024]{3,2,1,0:T(4,128)(2,1)} %bitcast.120), calls=%async_computation.1 | async-start | bytes 4194304 | tf_op jit(solution)/shard_map/all_to_all | solution.py:137
  75.1 3.5 %maximum_select_fusion = bf16[3,384,1024]{2,1,0:T(8,128)(2,1)} fusion(bf16[1,192,1024]{2,1,0:T(8,128)(2,1)S(1)} %bitcast.124, bf16[1,192,1024]{2,1,0:T(8,128)(2,1)S(1)} %bitcast.126, bf16[1,192,1024]{2,1,0:T(8,128)(2,1)} %bitcast.128, bf16[3,192,1024]{2,1,0:T(8,128)(2,1)} %collective-permute-done, pred[]{:T(512)S(6)} %eq.35), kind=kLoop, calls=%fused_computation.30 | loop fusion | flops 20054016 | bytes 4718593 | tf_op jit(solution)/shard_map/jit(_where)/select_n | solution.py:126
  78.6 36.6 %all-to-all-done.1 = bf16[16,16,4,1024]{3,2,1,0:T(4,128)(2,1)S(1)} async-done(((bf16[16,16,4,1024]{3,2,1,0:T(4,128)(2,1)}), bf16[16,16,4,1024]{3,2,1,0:T(4,128)(2,1)S(1)}, u32[]{:S(2)}, u32[]{:S(2)}) %all-to-all-start.1) | async-done | bytes 2097184 | tf_op jit(solution)/shard_map/all_to_all | solution.py:137
  117.2 3.2 %fusion.22 = f32[1024,384]{1,0:T(8,128)S(1)} fusion(bf16[1024,1024]{1,0:T(8,128)(2,1)} %reshape.284, bf16[3,384,1024]{2,1,0:T(8,128)(2,1)} %maximum_select_fusion), kind=kOutput, calls=%fused_computation.40 | convolution fusion | flops 805306368 | bytes 4456448 | tf_op jit(solution)/shard_map/dot_general | solution.py:16
  125.1 3.7 %convolution_convert_fusion = bf16[16,16,4,1024]{3,1,2,0:T(8,128)(2,1)} fusion(bf16[3,384,1024]{2,1,0:T(8,128)(2,1)S(1)} %copy-done.2, bf16[16,16,4,384]{3,2,1,0:T(4,128)(2,1)} %dot_general.22), kind=kOutput, calls=%fused_computation.31 | convolution fusion | flops 806354944 | bytes 3670016 | tf_op jit(solution)/shard_map/dot_general | solution.py:19
  128.8 6.7 %all-to-all-start.2 = ((bf16[16,16,4,1024]{3,1,2,0:T(8,128)(2,1)}), bf16[16,16,4,1024]{3,1,2,0:T(8,128)(2,1)S(1)}, u32[]{:S(2)}, u32[]{:S(2)}) async-start(bf16[16,16,4,1024]{3,1,2,0:T(8,128)(2,1)} %convolution_convert_fusion), calls=%async_computation.2 | async-start | bytes 4194304 | tf_op jit(solution)/shard_map/all_to_all | solution.py:139
  139.9 43.0 %all-to-all-done.2 = bf16[16,16,4,1024]{3,1,2,0:T(8,128)(2,1)S(1)} async-done(((bf16[16,16,4,1024]{3,1,2,0:T(8,128)(2,1)}), bf16[16,16,4,1024]{3,1,2,0:T(8,128)(2,1)S(1)}, u32[]{:S(2)}, u32[]{:S(2)}) %all-to-all-start.2) | async-done | bytes 2097184 | tf_op jit(solution)/shard_map/all_to_all | solution.py:139
  187.7 5.3 %all-to-all-start.3 = ((bf16[4,32,4,1024]{3,2,0,1:T(4,128)(2,1)}), bf16[4,32,4,1024]{3,2,0,1:T(4,128)(2,1)S(1)}, u32[]{:S(2)}, u32[]{:S(2)}) async-start(bf16[4,32,4,1024]{3,2,0,1:T(4,128)(2,1)} %copy.88), calls=%async_computation.3 | async-start | bytes 2097152 | tf_op jit(solution)/shard_map/all_to_all | solution.py:146
  193.1 14.3 %all-gather.5.cloned.1.call-done = bf16[1,4096,2,128]{3,1,2,0:T(8,128)(2,1)} async-done(((bf16[1,128,2,128]{3,1,2,0:T(8,128)(2,1)}), bf16[1,4096,2,128]{3,1,2,0:T(8,128)(2,1)}) %all-gather.5.cloned.1.call-update) | async-done | bytes 2097168 | tf_op jit(solution)/shard_map/all_gather | solution.py:38
  207.4 89.6 %while.15 = (s32[]{:T(128)}, f32[2,8,128]{2,1,0:T(8,128)S(1)}, f32[2,8,128]{2,1,0:T(8,128)S(1)}, f32[2,8,128,128]{3,2,1,0:T(8,128)S(1)}, s32[8]{0:T(128)S(1)}, /...) while((s32[]{:T(128)}, f32[2,8,128]{2,1,0:T(8,128)S(1)}, ...), condition=%wide.region_3.4_spmd.clone, body=%wide.region_0.3_spmd.clone.sunk | while | flops 551365248 | bytes 32904396 | solution.py:67
  208.8 3.7 %fusion.58 = (f32[2,8,128]{2,1,0:T(8,128)S(1)}, f32[2,512,128,8]{2,1,3,0:T(8,128)}) fusion(pred[128,512]{0,1:T(8,128)(4,1)S(1)} %broadcast_compare_fusion.2, bf16[128,2,8,128]{3,0,2,1:T(8,128)(2,1)S(1)} %get-tuple-element.236, bf16[8,512,2,128]{3,1,0,2:T(8,128)(2,1)} %get-tuple-element.235, s32[]{:T(128)S(6)} %copy.107), kind=kOutput, calls=%fused_computation.6.clone.1 | convolution fusion | flops 271579136 | bytes 5054468 | tf_op jit(solution)/shard_map/while/body/eval_jaxpr/qhgd,khd->hgqk/dot_general | solution.py:49
  212.5 3.3 %fusion.59 = f32[2,8,128]{2,1,0:T(8,128)S(1)} fusion(f32[2,512,128,8]{2,1,3,0:T(8,128)} %get-tuple-element.203, f32[2,8,128]{2,1,0:T(8,128)S(1)} %select_maximum_fusion.2, pred[128,512]{0,1:T(8,128)(4,1)S(1)} %broadcast_compare_fusion.2), kind=kLoop, calls=%fused_computation.8.clone.1 | loop fusion | flops 5240832 | bytes 4276224 | tf_op jit(solution)/shard_map/while/body/eval_jaxpr/reduce_sum | solution.py:58
  216.0 2.6 fusion.61
  220.0 3.7 %fusion.58 = (f32[2,8,128]{2,1,0:T(8,128)S(1)}, f32[2,512,128,8]{2,1,3,0:T(8,128)}) fusion(pred[128,512]{0,1:T(8,128)(4,1)S(1)} %broadcast_compare_fusion.2, bf16[128,2,8,128]{3,0,2,1:T(8,128)(2,1)S(1)} %get-tuple-element.236, bf16[8,512,2,128]{3,1,0,2:T(8,128)(2,1)} %get-tuple-element.235, s32[]{:T(128)S(6)} %copy.107), kind=kOutput, calls=%fused_computation.6.clone.1 | convolution fusion | flops 271579136 | bytes 5054468 | tf_op jit(solution)/shard_map/while/body/eval_jaxpr/qhgd,khd->hgqk/dot_general | solution.py:49
  223.7 3.3 %fusion.59 = f32[2,8,128]{2,1,0:T(8,128)S(1)} fusion(f32[2,512,128,8]{2,1,3,0:T(8,128)} %get-tuple-element.203, f32[2,8,128]{2,1,0:T(8,128)S(1)} %select_maximum_fusion.2, pred[128,512]{0,1:T(8,128)(4,1)S(1)} %broadcast_compare_fusion.2), kind=kLoop, calls=%fused_computation.8.clone.1 | loop fusion | flops 5240832 | bytes 4276224 | tf_op jit(solution)/shard_map/while/body/eval_jaxpr/reduce_sum | solution.py:58
  227.2 2.6 fusion.61
  231.2 3.7 %fusion.58 = (f32[2,8,128]{2,1,0:T(8,128)S(1)}, f32[2,512,128,8]{2,1,3,0:T(8,128)}) fusion(pred[128,512]{0,1:T(8,128)(4,1)S(1)} %broadcast_compare_fusion.2, bf16[128,2,8,128]{3,0,2,1:T(8,128)(2,1)S(1)} %get-tuple-element.236, bf16[8,512,2,128]{3,1,0,2:T(8,128)(2,1)} %get-tuple-element.235, s32[]{:T(128)S(6)} %copy.107), kind=kOutput, calls=%fused_computation.6.clone.1 | convolution fusion | flops 271579136 | bytes 5054468 | tf_op jit(solution)/shard_map/while/body/eval_jaxpr/qhgd,khd->hgqk/dot_general | solution.py:49
  234.9 3.3 %fusion.59 = f32[2,8,128]{2,1,0:T(8,128)S(1)} fusion(f32[2,512,128,8]{2,1,3,0:T(8,128)} %get-tuple-element.203, f32[2,8,128]{2,1,0:T(8,128)S(1)} %select_maximum_fusion.2, pred[128,512]{0,1:T(8,128)(4,1)S(1)} %broadcast_compare_fusion.2), kind=kLoop, calls=%fused_computation.8.clone.1 | loop fusion | flops 5240832 | bytes 4276224 | tf_op jit(solution)/shard_map/while/body/eval_jaxpr/reduce_sum | solution.py:58
  238.4 2.6 fusion.61
  242.5 3.7 %fusion.58 = (f32[2,8,128]{2,1,0:T(8,128)S(1)}, f32[2,512,128,8]{2,1,3,0:T(8,128)}) fusion(pred[128,512]{0,1:T(8,128)(4,1)S(1)} %broadcast_compare_fusion.2, bf16[128,2,8,128]{3,0,2,1:T(8,128)(2,1)S(1)} %get-tuple-element.236, bf16[8,512,2,128]{3,1,0,2:T(8,128)(2,1)} %get-tuple-element.235, s32[]{:T(128)S(6)} %copy.107), kind=kOutput, calls=%fused_computation.6.clone.1 | convolution fusion | flops 271579136 | bytes 5054468 | tf_op jit(solution)/shard_map/while/body/eval_jaxpr/qhgd,khd->hgqk/dot_general | solution.py:49
  246.1 3.3 %fusion.59 = f32[2,8,128]{2,1,0:T(8,128)S(1)} fusion(f32[2,512,128,8]{2,1,3,0:T(8,128)} %get-tuple-element.203, f32[2,8,128]{2,1,0:T(8,128)S(1)} %select_maximum_fusion.2, pred[128,512]{0,1:T(8,128)(4,1)S(1)} %broadcast_compare_fusion.2), kind=kLoop, calls=%fused_computation.8.clone.1 | loop fusion | flops 5240832 | bytes 4276224 | tf_op jit(solution)/shard_map/while/body/eval_jaxpr/reduce_sum | solution.py:58
  253.7 3.7 %fusion.58 = (f32[2,8,128]{2,1,0:T(8,128)S(1)}, f32[2,512,128,8]{2,1,3,0:T(8,128)}) fusion(pred[128,512]{0,1:T(8,128)(4,1)S(1)} %broadcast_compare_fusion.2, bf16[128,2,8,128]{3,0,2,1:T(8,128)(2,1)S(1)} %get-tuple-element.236, bf16[8,512,2,128]{3,1,0,2:T(8,128)(2,1)} %get-tuple-element.235, s32[]{:T(128)S(6)} %copy.107), kind=kOutput, calls=%fused_computation.6.clone.1 | convolution fusion | flops 271579136 | bytes 5054468 | tf_op jit(solution)/shard_map/while/body/eval_jaxpr/qhgd,khd->hgqk/dot_general | solution.py:49
  257.3 3.3 %fusion.59 = f32[2,8,128]{2,1,0:T(8,128)S(1)} fusion(f32[2,512,128,8]{2,1,3,0:T(8,128)} %get-tuple-element.203, f32[2,8,128]{2,1,0:T(8,128)S(1)} %select_maximum_fusion.2, pred[128,512]{0,1:T(8,128)(4,1)S(1)} %broadcast_compare_fusion.2), kind=kLoop, calls=%fused_computation.8.clone.1 | loop fusion | flops 5240832 | bytes 4276224 | tf_op jit(solution)/shard_map/while/body/eval_jaxpr/reduce_sum | solution.py:58
  264.9 3.7 %fusion.58 = (f32[2,8,128]{2,1,0:T(8,128)S(1)}, f32[2,512,128,8]{2,1,3,0:T(8,128)}) fusion(pred[128,512]{0,1:T(8,128)(4,1)S(1)} %broadcast_compare_fusion.2, bf16[128,2,8,128]{3,0,2,1:T(8,128)(2,1)S(1)} %get-tuple-element.236, bf16[8,512,2,128]{3,1,0,2:T(8,128)(2,1)} %get-tuple-element.235, s32[]{:T(128)S(6)} %copy.107), kind=kOutput, calls=%fused_computation.6.clone.1 | convolution fusion | flops 271579136 | bytes 5054468 | tf_op jit(solution)/shard_map/while/body/eval_jaxpr/qhgd,khd->hgqk/dot_general | solution.py:49
  268.6 3.3 %fusion.59 = f32[2,8,128]{2,1,0:T(8,128)S(1)} fusion(f32[2,512,128,8]{2,1,3,0:T(8,128)} %get-tuple-element.203, f32[2,8,128]{2,1,0:T(8,128)S(1)} %select_maximum_fusion.2, pred[128,512]{0,1:T(8,128)(4,1)S(1)} %broadcast_compare_fusion.2), kind=kLoop, calls=%fused_computation.8.clone.1 | loop fusion | flops 5240832 | bytes 4276224 | tf_op jit(solution)/shard_map/while/body/eval_jaxpr/reduce_sum | solution.py:58
  272.0 2.6 fusion.61
  276.1 3.7 %fusion.58 = (f32[2,8,128]{2,1,0:T(8,128)S(1)}, f32[2,512,128,8]{2,1,3,0:T(8,128)}) fusion(pred[128,512]{0,1:T(8,128)(4,1)S(1)} %broadcast_compare_fusion.2, bf16[128,2,8,128]{3,0,2,1:T(8,128)(2,1)S(1)} %get-tuple-element.236, bf16[8,512,2,128]{3,1,0,2:T(8,128)(2,1)} %get-tuple-element.235, s32[]{:T(128)S(6)} %copy.107), kind=kOutput, calls=%fused_computation.6.clone.1 | convolution fusion | flops 271579136 | bytes 5054468 | tf_op jit(solution)/shard_map/while/body/eval_jaxpr/qhgd,khd->hgqk/dot_general | solution.py:49
  279.8 3.3 %fusion.59 = f32[2,8,128]{2,1,0:T(8,128)S(1)} fusion(f32[2,512,128,8]{2,1,3,0:T(8,128)} %get-tuple-element.203, f32[2,8,128]{2,1,0:T(8,128)S(1)} %select_maximum_fusion.2, pred[128,512]{0,1:T(8,128)(4,1)S(1)} %broadcast_compare_fusion.2), kind=kLoop, calls=%fused_computation.8.clone.1 | loop fusion | flops 5240832 | bytes 4276224 | tf_op jit(solution)/shard_map/while/body/eval_jaxpr/reduce_sum | solution.py:58
  287.3 3.7 %fusion.58 = (f32[2,8,128]{2,1,0:T(8,128)S(1)}, f32[2,512,128,8]{2,1,3,0:T(8,128)}) fusion(pred[128,512]{0,1:T(8,128)(4,1)S(1)} %broadcast_compare_fusion.2, bf16[128,2,8,128]{3,0,2,1:T(8,128)(2,1)S(1)} %get-tuple-element.236, bf16[8,512,2,128]{3,1,0,2:T(8,128)(2,1)} %get-tuple-element.235, s32[]{:T(128)S(6)} %copy.107), kind=kOutput, calls=%fused_computation.6.clone.1 | convolution fusion | flops 271579136 | bytes 5054468 | tf_op jit(solution)/shard_map/while/body/eval_jaxpr/qhgd,khd->hgqk/dot_general | solution.py:49
  291.0 3.3 %fusion.59 = f32[2,8,128]{2,1,0:T(8,128)S(1)} fusion(f32[2,512,128,8]{2,1,3,0:T(8,128)} %get-tuple-element.203, f32[2,8,128]{2,1,0:T(8,128)S(1)} %select_maximum_fusion.2, pred[128,512]{0,1:T(8,128)(4,1)S(1)} %broadcast_compare_fusion.2), kind=kLoop, calls=%fused_computation.8.clone.1 | loop fusion | flops 5240832 | bytes 4276224 | tf_op jit(solution)/shard_map/while/body/eval_jaxpr/reduce_sum | solution.py:58
  (162 shorter events, 58.7 us)
Async XLA Ops:
  7.2 130.2 %copy-start = (bf16[1024,128]{1,0:T(8,128)(2,1)S(1)}, bf16[1024,128]{1,0:T(8,128)(2,1)}, u32[]{:S(2)}) copy-start(bf16[1024,128]{1,0:T(8,128)(2,1)} %param.18) | copy-start | bytes 786436
  14.8 14.8 %copy-start.7 = (bf16[1,128,2,128]{3,2,1,0:T(2,128)(2,1)S(1)}, bf16[1,128,2,128]{3,2,1,0:T(2,128)(2,1)}, u32[]{:S(2)}) copy-start(bf16[1,128,2,128]{3,2,1,0:T(2,128)(2,1)} %param.14) | copy-start | bytes 196612
  16.4 41.3 %all-to-all-start = ((bf16[4,32,4,1024]{3,2,0,1:T(4,128)(2,1)}), bf16[4,32,4,1024]{3,2,0,1:T(4,128)(2,1)S(1)}, u32[]{:S(2)}, u32[]{:S(2)}) async-start(bf16[4,32,4,1024]{3,2,0,1:T(4,128)(2,1)} %copy.84), calls=%async_computation | async-start | bytes 2097152 | tf_op jit(solution)/shard_map/all_to_all | solution.py:121
  29.5 163.6 %all-gather.3.cloned.1.call-start = ((), (), s32[]{:S(2)}) async-start(), calls=%async_computation.4 | async-start | bytes 2162688 | tf_op jit(solution)/shard_map/all_gather | solution.py:37
  60.2 7.6 %copy-start.4 = (bf16[192,1024]{1,0:T(8,128)(2,1)S(1)}, bf16[192,1024]{1,0:T(8,128)(2,1)}, u32[]{:S(2)}) copy-start(bf16[192,1024]{1,0:T(8,128)(2,1)} %param.21) | copy-start | bytes 1179652
  60.2 7.6 %copy-start.5 = (bf16[192,1024]{1,0:T(8,128)(2,1)S(1)}, bf16[192,1024]{1,0:T(8,128)(2,1)}, u32[]{:S(2)}) copy-start(bf16[192,1024]{1,0:T(8,128)(2,1)} %param.20) | copy-start | bytes 1179652
  60.2 11.9 %copy-start.8 = (bf16[1,128,2,128]{3,2,1,0:T(2,128)(2,1)S(1)}, bf16[1,128,2,128]{3,2,1,0:T(2,128)(2,1)}, u32[]{:S(2)}) copy-start(bf16[1,128,2,128]{3,2,1,0:T(2,128)(2,1)} %param.15) | copy-start | bytes 196612
  60.2 55.0 %all-to-all-start.1 = ((bf16[16,16,4,1024]{3,2,1,0:T(4,128)(2,1)}), bf16[16,16,4,1024]{3,2,1,0:T(4,128)(2,1)S(1)}, u32[]{:S(2)}, u32[]{:S(2)}) async-start(bf16[16,16,4,1024]{3,2,1,0:T(4,128)(2,1)} %bitcast.120), calls=%async_computation.1 | async-start | bytes 4194304 | tf_op jit(solution)/shard_map/all_to_all | solution.py:137
  67.8 139.7 %all-gather.5.cloned.1.call-start = ((), (), s32[]{:S(2)}) async-start(), calls=%async_computation.5 | async-start | bytes 2162688 | tf_op jit(solution)/shard_map/all_gather | solution.py:38
  70.0 5.1 %collective-permute-start = (bf16[3,192,1024]{2,1,0:T(8,128)(2,1)}, bf16[3,192,1024]{2,1,0:T(8,128)(2,1)}, u32[]{:S(2)}, u32[]{:S(2)}) collective-permute-start(bf16[3,192,1024]{2,1,0:T(8,128)(2,1)} %pad_maximum_fusion), channel_id=1, source_target_pairs={{0,1},{1,0},{2,3},{3,2},{4,5},{5,4},{6,7},{7,6},{8,9},{9,8},{10,11... | collective-permute-start | bytes 3538952 | tf_op jit(solution)/shard_map/ppermute | solution.py:9
  117.2 3.2 %copy-start.2 = (bf16[3,384,1024]{2,1,0:T(8,128)(2,1)S(1)}, bf16[3,384,1024]{2,1,0:T(8,128)(2,1)}, u32[]{:S(2)}) copy-start(bf16[3,384,1024]{2,1,0:T(8,128)(2,1)} %maximum_select_fusion) | copy-start | bytes 7077892
  117.2 3.2 %copy-start.3 = (bf16[1024,1024]{1,0:T(8,128)(2,1)S(1)}, bf16[1024,1024]{1,0:T(8,128)(2,1)}, u32[]{:S(2)}) copy-start(bf16[1024,1024]{1,0:T(8,128)(2,1)} %reshape.284) | copy-start | bytes 6291460
  128.8 8.1 %copy-start.9 = (s32[1,128,2]{1,2,0:T(2,128)S(1)}, s32[1,128,2]{1,2,0:T(2,128)}, u32[]{:S(2)}) copy-start(s32[1,128,2]{1,2,0:T(2,128)} %param.16) | copy-start | bytes 3076
  128.8 54.1 %all-to-all-start.2 = ((bf16[16,16,4,1024]{3,1,2,0:T(8,128)(2,1)}), bf16[16,16,4,1024]{3,1,2,0:T(8,128)(2,1)S(1)}, u32[]{:S(2)}, u32[]{:S(2)}) async-start(bf16[16,16,4,1024]{3,1,2,0:T(8,128)(2,1)} %convolution_convert_fusion), calls=%async_computation.2 | async-start | bytes 4194304 | tf_op jit(solution)/shard_map/all_to_all | solution.py:139
  185.9 21.5 %copy-start.6 = (f32[2,8,128,128]{3,2,1,0:T(8,128)S(1)}, f32[2,8,128,128]{3,2,1,0:T(8,128)}, u32[]{:S(2)}) copy-start(f32[2,8,128,128]{3,2,1,0:T(8,128)} %custom-call.4) | copy-start | bytes 3145732
  187.7 110.8 %all-to-all-start.3 = ((bf16[4,32,4,1024]{3,2,0,1:T(4,128)(2,1)}), bf16[4,32,4,1024]{3,2,0,1:T(4,128)(2,1)S(1)}, u32[]{:S(2)}, u32[]{:S(2)}) async-start(bf16[4,32,4,1024]{3,2,0,1:T(4,128)(2,1)} %copy.88), calls=%async_computation.3 | async-start | bytes 2097152 | tf_op jit(solution)/shard_map/all_to_all | solution.py:146
  212.5 3.4 %copy-start.1 = (f32[2,512,128,8]{2,1,3,0:T(8,128)S(1)}, f32[2,512,128,8]{2,1,3,0:T(8,128)}, u32[]{:S(2)}) copy-start(f32[2,512,128,8]{2,1,3,0:T(8,128)} %get-tuple-element.203) | copy-start | bytes 12582916 | tf_op jit(solution)/shard_map/while
  223.7 3.4 %copy-start.1 = (f32[2,512,128,8]{2,1,3,0:T(8,128)S(1)}, f32[2,512,128,8]{2,1,3,0:T(8,128)}, u32[]{:S(2)}) copy-start(f32[2,512,128,8]{2,1,3,0:T(8,128)} %get-tuple-element.203) | copy-start | bytes 12582916 | tf_op jit(solution)/shard_map/while
  234.9 3.4 %copy-start.1 = (f32[2,512,128,8]{2,1,3,0:T(8,128)S(1)}, f32[2,512,128,8]{2,1,3,0:T(8,128)}, u32[]{:S(2)}) copy-start(f32[2,512,128,8]{2,1,3,0:T(8,128)} %get-tuple-element.203) | copy-start | bytes 12582916 | tf_op jit(solution)/shard_map/while
  246.1 3.4 %copy-start.1 = (f32[2,512,128,8]{2,1,3,0:T(8,128)S(1)}, f32[2,512,128,8]{2,1,3,0:T(8,128)}, u32[]{:S(2)}) copy-start(f32[2,512,128,8]{2,1,3,0:T(8,128)} %get-tuple-element.203) | copy-start | bytes 12582916 | tf_op jit(solution)/shard_map/while
  257.3 3.4 %copy-start.1 = (f32[2,512,128,8]{2,1,3,0:T(8,128)S(1)}, f32[2,512,128,8]{2,1,3,0:T(8,128)}, u32[]{:S(2)}) copy-start(f32[2,512,128,8]{2,1,3,0:T(8,128)} %get-tuple-element.203) | copy-start | bytes 12582916 | tf_op jit(solution)/shard_map/while
  268.5 3.4 %copy-start.1 = (f32[2,512,128,8]{2,1,3,0:T(8,128)S(1)}, f32[2,512,128,8]{2,1,3,0:T(8,128)}, u32[]{:S(2)}) copy-start(f32[2,512,128,8]{2,1,3,0:T(8,128)} %get-tuple-element.203) | copy-start | bytes 12582916 | tf_op jit(solution)/shard_map/while
  279.7 3.4 %copy-start.1 = (f32[2,512,128,8]{2,1,3,0:T(8,128)S(1)}, f32[2,512,128,8]{2,1,3,0:T(8,128)}, u32[]{:S(2)}) copy-start(f32[2,512,128,8]{2,1,3,0:T(8,128)} %get-tuple-element.203) | copy-start | bytes 12582916 | tf_op jit(solution)/shard_map/while
  290.9 3.4 %copy-start.1 = (f32[2,512,128,8]{2,1,3,0:T(8,128)S(1)}, f32[2,512,128,8]{2,1,3,0:T(8,128)}, u32[]{:S(2)}) copy-start(f32[2,512,128,8]{2,1,3,0:T(8,128)} %get-tuple-element.203) | copy-start | bytes 12582916 | tf_op jit(solution)/shard_map/while
Sparse Core Ops, SparseCore 0:
  34.1 84.8 all-gather.2
  122.8 84.6 all-gather.4
where the time goes:
time: 311 us; the launch traced here: 310 us
  waiting for transfers between devices  124 us (40%)
  matrix products  60 us (19%)
  other arithmetic  41.4 us (13%)
  starting transfers between devices  34.9 us (11%)
  local copies, waits for them, and re-layouts  29.7 us (10%)
  between operations  14.4 us (5%)
  loops' own time  5.69 us (2%)
    all_to_all x1, waiting for transfers between devices, local(): lax.all_to_all(partials.astype(jnp.bfloat16), 'exp', split_axis=0, concat...  43 us
    all_to_all x1, waiting for transfers between devices, local(): lax.all_to_all(spread_rows, 'exp', split_axis=0, concat_axis=0, tiled=True)  36.6 us
    dot_general x8, matrix products, advance(): jnp.einsum('qhgd,khd->hgqk', grouped, key_block, preferred_element_type=j...  29.5 us
    all_to_all x1, waiting for transfers between devices, local(): lax.all_to_all(outgoing, 'ctx', split_axis=1, concat_axis=1, tiled=True)  27.4 us
    reduce_sum x8, other arithmetic, advance(): totals = totals * factor + jnp.sum(weights, axis=-1)  26.6 us
    dot_general x8, matrix products, advance(): jnp.einsum('hgqk,khd->hgqd', weights.astype(jnp.bfloat16), value_block, p...  21.1 us
    all_gather x1, waiting for transfers between devices, attention(): value_piece = lax.all_gather(value_rows, 'ctx', axis=1, tiled=True)  14.3 us
    all_to_all x1, starting transfers between devices, local(): lax.all_to_all(outgoing, 'ctx', split_axis=1, concat_axis=1, tiled=True)  13.2 us
  transfers between devices with their start and end apart: 7, of which 5 were waited for; matrix products, arithmetic and copies ran while one was open for 38% of the time, Pallas kernels for 0%

commit v1 on v0

--- a/solution.py
+++ b/solution.py
@@ -134,7 +134,23 @@
         halves_rows, (per_ctx, quarters // 2, 2, half_ctx, capacity, features)
     )
     spread_rows = spread_rows.reshape(exp_count, half_ctx, capacity, features)
-    received = lax.all_to_all(spread_rows, "exp", split_axis=0, concat_axis=0, tiled=True)
+    left_arr = lax.axis_size("exp")
+    now, state_now = (left_arr, lax.axis_index("exp"))
+    res = spread_rows.shape[0] // now
+    heard = list(spread_rows.shape)
+    heard[0] = res
+    long_array = heard[0]
+    heard[0] = long_array * now
+    m = 0
+    received = jnp.zeros(heard, spread_rows.dtype)
+    while m < now:
+        before = lax.dynamic_slice_in_dim(spread_rows, (state_now ^ m) * res, res, axis=0)
+        if m:
+            before = lax.ppermute(before, axis_name="exp", perm=[(kk, kk ^ m) for kk in range(now)])
+        received = lax.dynamic_update_slice_in_dim(
+            received, before, (state_now ^ m) * long_array, axis=0
+        )
+        m = m + 1
     partials = expert_rows(received, held[0], held[1], held[2])
     returned = lax.all_to_all(
         partials.astype(jnp.bfloat16), "exp", split_axis=0, concat_axis=0, tiled=True

time: 311 us -> 337 us (1.084)
  the two profiles are of different devices: /device:TPU:16 before, /device:TPU:1 now
where the time goes in v1:
time: 337 us; the launch traced here: 335 us
  starting transfers between devices  102 us (30%)
  waiting for transfers between devices  80.4 us (24%)
  matrix products  60.2 us (18%)
  other arithmetic  40.3 us (12%)
  local copies, waits for them, and re-layouts  32.5 us (10%)
  between operations  14.8 us (4%)
  loops' own time  5.71 us (2%)
    ppermute x15, starting transfers between devices, local(): lax.ppermute(before, axis_name='exp', perm=[(kk, kk ^ m) for kk in range(...  71.1 us
    all_to_all x1, waiting for transfers between devices, local(): lax.all_to_all(partials.astype(jnp.bfloat16), 'exp', split_axis=0, concat...  44.6 us
    dot_general x8, matrix products, advance(): jnp.einsum('qhgd,khd->hgqk', grouped, key_block, preferred_element_type=j...  29.6 us
    reduce_sum x8, other arithmetic, advance(): totals = totals * factor + jnp.sum(weights, axis=-1)  26.6 us
    all_to_all x1, waiting for transfers between devices, local(): lax.all_to_all(outgoing, 'ctx', split_axis=1, concat_axis=1, tiled=True)  23.2 us
    dot_general x8, matrix products, advance(): jnp.einsum('hgqk,khd->hgqd', weights.astype(jnp.bfloat16), value_block, p...  21.1 us
    all_to_all x1, starting transfers between devices, local(): lax.all_to_all(outgoing, 'ctx', split_axis=1, concat_axis=1, tiled=True)  13.8 us
    ppermute x15, waiting for transfers between devices, local(): lax.ppermute(before, axis_name='exp', perm=[(kk, kk ^ m) for kk in range(...  12.6 us
  transfers between devices with their start and end apart: 21, of which 5 were waited for; matrix products, arithmetic and copies ran while one was open for 38% of the time, Pallas kernels for 0%

profile of v1, /device:TPU:1, one launch (start us, length us, event | category | flops | bytes accessed | tf_op | source)
XLA Modules:
  0.0 335.5 jit_solution(6848522568322075552)
XLA Ops:
  17.9 13.8 %all-to-all-start = ((bf16[4,32,4,1024]{3,2,0,1:T(4,128)(2,1)}), bf16[4,32,4,1024]{3,2,0,1:T(4,128)(2,1)S(1)}, u32[]{:S(2)}, u32[]{:S(2)}) async-start(bf16[4,32,4,1024]{3,2,0,1:T(4,128)(2,1)} %copy.84), calls=%async_computation | async-start | bytes 2097152 | tf_op jit(solution)/shard_map/all_to_all | solution.py:121
  36.6 23.2 %all-to-all-done = bf16[4,32,4,1024]{3,2,0,1:T(4,128)(2,1)S(1)} async-done(((bf16[4,32,4,1024]{3,2,0,1:T(4,128)(2,1)}), bf16[4,32,4,1024]{3,2,0,1:T(4,128)(2,1)S(1)}, u32[]{:S(2)}, u32[]{:S(2)}) %all-to-all-start) | async-done | bytes 1048608 | tf_op jit(solution)/shard_map/all_to_all | solution.py:121
  63.2 5.1 %collective-permute-start = (bf16[1,16,4,1024]{3,2,1,0:T(4,128)(2,1)S(1)}, bf16[1,16,4,1024]{3,2,1,0:T(4,128)(2,1)S(1)}, u32[]{:S(2)}, u32[]{:S(2)}) collective-permute-start(bf16[1,16,4,1024]{3,2,1,0:T(4,128)(2,1)S(1)} %get-tuple-element.157), channel_id=1, source_target_pairs={{0,1},{1,0},{2,3},{3,2},{4,5},{5,4},{6,7},{7,6},{8,9},{9,8},{10,11... | collective-permute-start | bytes 393224 | tf_op jit(solution)/shard_map/ppermute | solution.py:149
  71.5 3.4 %maximum_select_fusion = bf16[3,384,1024]{2,1,0:T(8,128)(2,1)} fusion(bf16[1,192,1024]{2,1,0:T(8,128)(2,1)S(1)} %bitcast.126, bf16[1,192,1024]{2,1,0:T(8,128)(2,1)S(1)} %bitcast.128, bf16[1,192,1024]{2,1,0:T(8,128)(2,1)S(1)} %bitcast.130, bf16[3,192,1024]{2,1,0:T(8,128)(2,1)} %collective-permute-done.15, pred[]{:T(512)S(6)} %eq.35), kind=kLoop, calls=%fused_computation.30 | loop fusion | flops 20054016 | bytes 4718593 | tf_op jit(solution)/shard_map/jit(_where)/select_n | solution.py:126
  77.1 4.2 %collective-permute-start.3 = (bf16[1,16,4,1024]{3,2,1,0:T(4,128)(2,1)S(1)}, bf16[1,16,4,1024]{3,2,1,0:T(4,128)(2,1)S(1)}, u32[]{:S(2)}, u32[]{:S(2)}) collective-permute-start(bf16[1,16,4,1024]{3,2,1,0:T(4,128)(2,1)S(1)} %get-tuple-element.154), channel_id=1, source_target_pairs={{0,4},{1,5},{2,6},{3,7},{4,0},{5,1},{6,2},{7,3},{8,12},{9,13},{10,... | collective-permute-start | bytes 393224 | tf_op jit(solution)/shard_map/ppermute | solution.py:149
  83.7 5.3 %collective-permute-start.5 = (bf16[1,16,4,1024]{3,2,1,0:T(4,128)(2,1)S(1)}, bf16[1,16,4,1024]{3,2,1,0:T(4,128)(2,1)S(1)}, u32[]{:S(2)}, u32[]{:S(2)}) collective-permute-start(bf16[1,16,4,1024]{3,2,1,0:T(4,128)(2,1)S(1)} %get-tuple-element.152), channel_id=1, source_target_pairs={{0,6},{1,7},{2,4},{3,5},{4,2},{5,3},{6,0},{7,1},{8,14},{9,15},{10,... | collective-permute-start | bytes 393224 | tf_op jit(solution)/shard_map/ppermute | solution.py:149
  91.2 7.4 %collective-permute-start.7 = (bf16[1,16,4,1024]{3,2,1,0:T(4,128)(2,1)S(1)}, bf16[1,16,4,1024]{3,2,1,0:T(4,128)(2,1)S(1)}, u32[]{:S(2)}, u32[]{:S(2)}) collective-permute-start(bf16[1,16,4,1024]{3,2,1,0:T(4,128)(2,1)S(1)} %get-tuple-element.150), channel_id=1, source_target_pairs={{0,8},{1,9},{2,10},{3,11},{4,12},{5,13},{6,14},{7,15},{8,0},{9,1},... | collective-permute-start | bytes 393224 | tf_op jit(solution)/shard_map/ppermute | solution.py:149
  98.7 6.1 %collective-permute-start.8 = (bf16[1,16,4,1024]{3,2,1,0:T(4,128)(2,1)S(1)}, bf16[1,16,4,1024]{3,2,1,0:T(4,128)(2,1)S(1)}, u32[]{:S(2)}, u32[]{:S(2)}) collective-permute-start(bf16[1,16,4,1024]{3,2,1,0:T(4,128)(2,1)S(1)} %get-tuple-element.149), channel_id=1, source_target_pairs={{0,9},{1,8},{2,11},{3,10},{4,13},{5,12},{6,15},{7,14},{8,1},{9,0},... | collective-permute-start | bytes 393224 | tf_op jit(solution)/shard_map/ppermute | solution.py:149
  106.9 16.7 %collective-permute-start.10 = (bf16[1,16,4,1024]{3,2,1,0:T(4,128)(2,1)S(1)}, bf16[1,16,4,1024]{3,2,1,0:T(4,128)(2,1)S(1)}, u32[]{:S(2)}, u32[]{:S(2)}) collective-permute-start(bf16[1,16,4,1024]{3,2,1,0:T(4,128)(2,1)S(1)} %get-tuple-element.147), channel_id=1, source_target_pairs={{0,11},{1,10},{2,9},{3,8},{4,15},{5,14},{6,13},{7,12},{8,3},{9,2},... | collective-permute-start | bytes 393224 | tf_op jit(solution)/shard_map/ppermute | solution.py:149
  123.6 3.9 %collective-permute-start.11 = (bf16[1,16,4,1024]{3,2,1,0:T(4,128)(2,1)S(1)}, bf16[1,16,4,1024]{3,2,1,0:T(4,128)(2,1)S(1)}, u32[]{:S(2)}, u32[]{:S(2)}) collective-permute-start(bf16[1,16,4,1024]{3,2,1,0:T(4,128)(2,1)S(1)} %get-tuple-element.146), channel_id=1, source_target_pairs={{0,12},{1,13},{2,14},{3,15},{4,8},{5,9},{6,10},{7,11},{8,4},{9,5},... | collective-permute-start | bytes 393224 | tf_op jit(solution)/shard_map/ppermute | solution.py:149
  132.9 5.6 %collective-permute-start.14 = (bf16[1,16,4,1024]{3,2,1,0:T(4,128)(2,1)S(1)}, bf16[1,16,4,1024]{3,2,1,0:T(4,128)(2,1)S(1)}, u32[]{:S(2)}, u32[]{:S(2)}) collective-permute-start(bf16[1,16,4,1024]{3,2,1,0:T(4,128)(2,1)S(1)} %get-tuple-element.143), channel_id=1, source_target_pairs={{0,15},{1,14},{2,13},{3,12},{4,11},{5,10},{6,9},{7,8},{8,7},{9,6},... | collective-permute-start | bytes 393224 | tf_op jit(solution)/shard_map/ppermute | solution.py:149
  138.7 5.6 %collective-permute-done.12 = bf16[1,16,4,1024]{3,2,1,0:T(4,128)(2,1)S(1)} collective-permute-done((bf16[1,16,4,1024]{3,2,1,0:T(4,128)(2,1)S(1)}, bf16[1,16,4,1024]{3,2,1,0:T(4,128)(2,1)S(1)}, u32[]{:S(2)}, u32[]{:S(2)}) %collective-permute-start.12) | collective-permute-done | bytes 131104 | tf_op jit(solution)/shard_map/ppermute | solution.py:149
  144.4 3.7 %collective-permute-done.13 = bf16[1,16,4,1024]{3,2,1,0:T(4,128)(2,1)S(1)} collective-permute-done((bf16[1,16,4,1024]{3,2,1,0:T(4,128)(2,1)S(1)}, bf16[1,16,4,1024]{3,2,1,0:T(4,128)(2,1)S(1)}, u32[]{:S(2)}, u32[]{:S(2)}) %collective-permute-start.13) | collective-permute-done | bytes 131104 | tf_op jit(solution)/shard_map/ppermute | solution.py:149
  161.5 3.7 %convolution_convert_fusion = bf16[16,16,4,1024]{3,1,2,0:T(8,128)(2,1)} fusion(bf16[3,384,1024]{2,1,0:T(8,128)(2,1)S(1)} %copy-done.2, bf16[16,16,4,384]{3,2,1,0:T(4,128)(2,1)} %dot_general.22), kind=kOutput, calls=%fused_computation.31 | convolution fusion | flops 806354944 | bytes 3670016 | tf_op jit(solution)/shard_map/dot_general | solution.py:19
  165.3 8.6 %all-to-all-start.1 = ((bf16[16,16,4,1024]{3,1,2,0:T(8,128)(2,1)}), bf16[16,16,4,1024]{3,1,2,0:T(8,128)(2,1)S(1)}, u32[]{:S(2)}, u32[]{:S(2)}) async-start(bf16[16,16,4,1024]{3,1,2,0:T(8,128)(2,1)} %convolution_convert_fusion), calls=%async_computation.1 | async-start | bytes 4194304 | tf_op jit(solution)/shard_map/all_to_all | solution.py:155
  178.2 44.6 %all-to-all-done.1 = bf16[16,16,4,1024]{3,1,2,0:T(8,128)(2,1)S(1)} async-done(((bf16[16,16,4,1024]{3,1,2,0:T(8,128)(2,1)}), bf16[16,16,4,1024]{3,1,2,0:T(8,128)(2,1)S(1)}, u32[]{:S(2)}, u32[]{:S(2)}) %all-to-all-start.1) | async-done | bytes 2097184 | tf_op jit(solution)/shard_map/all_to_all | solution.py:155
  227.7 5.1 %all-to-all-start.2 = ((bf16[4,32,4,1024]{3,2,0,1:T(4,128)(2,1)}), bf16[4,32,4,1024]{3,2,0,1:T(4,128)(2,1)S(1)}, u32[]{:S(2)}, u32[]{:S(2)}) async-start(bf16[4,32,4,1024]{3,2,0,1:T(4,128)(2,1)} %copy.88), calls=%async_computation.2 | async-start | bytes 2097152 | tf_op jit(solution)/shard_map/all_to_all | solution.py:162
  232.9 89.9 %while.15 = (s32[]{:T(128)}, f32[2,8,128]{2,1,0:T(8,128)S(1)}, f32[2,8,128]{2,1,0:T(8,128)S(1)}, f32[2,8,128,128]{3,2,1,0:T(8,128)S(1)}, s32[8]{0:T(128)S(1)}, /...) while((s32[]{:T(128)}, f32[2,8,128]{2,1,0:T(8,128)S(1)}, ...), condition=%wide.region_3.4_spmd.clone, body=%wide.region_0.3_spmd.clone.sunk | while | flops 551365248 | bytes 32905404 | solution.py:67
  234.3 3.7 %fusion.59 = (f32[2,8,128]{2,1,0:T(8,128)S(1)}, f32[2,512,128,8]{2,1,3,0:T(8,128)}) fusion(pred[128,512]{0,1:T(8,128)(4,1)S(1)} %broadcast_compare_fusion.2, bf16[128,2,8,128]{3,0,2,1:T(8,128)(2,1)S(1)} %get-tuple-element.252, bf16[8,512,2,128]{3,1,0,2:T(8,128)(2,1)} %get-tuple-element.251, s32[]{:T(128)} %get-tuple-element.234), kind=kOutput, calls=%fused_computation.6.clone.1 | convolution fusion | flops 271579136 | bytes 5054976 | tf_op jit(solution)/shard_map/while/body/eval_jaxpr/qhgd,khd->hgqk/dot_general | solution.py:49
  238.0 3.3 fusion.60
  245.5 3.7 %fusion.59 = (f32[2,8,128]{2,1,0:T(8,128)S(1)}, f32[2,512,128,8]{2,1,3,0:T(8,128)}) fusion(pred[128,512]{0,1:T(8,128)(4,1)S(1)} %broadcast_compare_fusion.2, bf16[128,2,8,128]{3,0,2,1:T(8,128)(2,1)S(1)} %get-tuple-element.252, bf16[8,512,2,128]{3,1,0,2:T(8,128)(2,1)} %get-tuple-element.251, s32[]{:T(128)} %get-tuple-element.234), kind=kOutput, calls=%fused_computation.6.clone.1 | convolution fusion | flops 271579136 | bytes 5054976 | tf_op jit(solution)/shard_map/while/body/eval_jaxpr/qhgd,khd->hgqk/dot_general | solution.py:49
  249.2 3.3 fusion.60
  256.7 3.7 %fusion.59 = (f32[2,8,128]{2,1,0:T(8,128)S(1)}, f32[2,512,128,8]{2,1,3,0:T(8,128)}) fusion(pred[128,512]{0,1:T(8,128)(4,1)S(1)} %broadcast_compare_fusion.2, bf16[128,2,8,128]{3,0,2,1:T(8,128)(2,1)S(1)} %get-tuple-element.252, bf16[8,512,2,128]{3,1,0,2:T(8,128)(2,1)} %get-tuple-element.251, s32[]{:T(128)} %get-tuple-element.234), kind=kOutput, calls=%fused_computation.6.clone.1 | convolution fusion | flops 271579136 | bytes 5054976 | tf_op jit(solution)/shard_map/while/body/eval_jaxpr/qhgd,khd->hgqk/dot_general | solution.py:49
  260.5 3.3 fusion.60
  268.0 3.7 %fusion.59 = (f32[2,8,128]{2,1,0:T(8,128)S(1)}, f32[2,512,128,8]{2,1,3,0:T(8,128)}) fusion(pred[128,512]{0,1:T(8,128)(4,1)S(1)} %broadcast_compare_fusion.2, bf16[128,2,8,128]{3,0,2,1:T(8,128)(2,1)S(1)} %get-tuple-element.252, bf16[8,512,2,128]{3,1,0,2:T(8,128)(2,1)} %get-tuple-element.251, s32[]{:T(128)} %get-tuple-element.234), kind=kOutput, calls=%fused_computation.6.clone.1 | convolution fusion | flops 271579136 | bytes 5054976 | tf_op jit(solution)/shard_map/while/body/eval_jaxpr/qhgd,khd->hgqk/dot_general | solution.py:49
  271.7 3.3 fusion.60
  279.2 3.7 %fusion.59 = (f32[2,8,128]{2,1,0:T(8,128)S(1)}, f32[2,512,128,8]{2,1,3,0:T(8,128)}) fusion(pred[128,512]{0,1:T(8,128)(4,1)S(1)} %broadcast_compare_fusion.2, bf16[128,2,8,128]{3,0,2,1:T(8,128)(2,1)S(1)} %get-tuple-element.252, bf16[8,512,2,128]{3,1,0,2:T(8,128)(2,1)} %get-tuple-element.251, s32[]{:T(128)} %get-tuple-element.234), kind=kOutput, calls=%fused_computation.6.clone.1 | convolution fusion | flops 271579136 | bytes 5054976 | tf_op jit(solution)/shard_map/while/body/eval_jaxpr/qhgd,khd->hgqk/dot_general | solution.py:49
  282.9 3.3 fusion.60
  290.4 3.7 %fusion.59 = (f32[2,8,128]{2,1,0:T(8,128)S(1)}, f32[2,512,128,8]{2,1,3,0:T(8,128)}) fusion(pred[128,512]{0,1:T(8,128)(4,1)S(1)} %broadcast_compare_fusion.2, bf16[128,2,8,128]{3,0,2,1:T(8,128)(2,1)S(1)} %get-tuple-element.252, bf16[8,512,2,128]{3,1,0,2:T(8,128)(2,1)} %get-tuple-element.251, s32[]{:T(128)} %get-tuple-element.234), kind=kOutput, calls=%fused_computation.6.clone.1 | convolution fusion | flops 271579136 | bytes 5054976 | tf_op jit(solution)/shard_map/while/body/eval_jaxpr/qhgd,khd->hgqk/dot_general | solution.py:49
  301.7 3.7 %fusion.59 = (f32[2,8,128]{2,1,0:T(8,128)S(1)}, f32[2,512,128,8]{2,1,3,0:T(8,128)}) fusion(pred[128,512]{0,1:T(8,128)(4,1)S(1)} %broadcast_compare_fusion.2, bf16[128,2,8,128]{3,0,2,1:T(8,128)(2,1)S(1)} %get-tuple-element.252, bf16[8,512,2,128]{3,1,0,2:T(8,128)(2,1)} %get-tuple-element.251, s32[]{:T(128)} %get-tuple-element.234), kind=kOutput, calls=%fused_computation.6.clone.1 | convolution fusion | flops 271579136 | bytes 5054976 | tf_op jit(solution)/shard_map/while/body/eval_jaxpr/qhgd,khd->hgqk/dot_general | solution.py:49
  312.9 3.7 %fusion.59 = (f32[2,8,128]{2,1,0:T(8,128)S(1)}, f32[2,512,128,8]{2,1,3,0:T(8,128)}) fusion(pred[128,512]{0,1:T(8,128)(4,1)S(1)} %broadcast_compare_fusion.2, bf16[128,2,8,128]{3,0,2,1:T(8,128)(2,1)S(1)} %get-tuple-element.252, bf16[8,512,2,128]{3,1,0,2:T(8,128)(2,1)} %get-tuple-element.251, s32[]{:T(128)} %get-tuple-element.234), kind=kOutput, calls=%fused_computation.6.clone.1 | convolution fusion | flops 271579136 | bytes 5054976 | tf_op jit(solution)/shard_map/while/body/eval_jaxpr/qhgd,khd->hgqk/dot_general | solution.py:49
  316.6 3.3 fusion.60
  (209 shorter events, 99.4 us)
Async XLA Ops:
  7.2 167.4 %copy-start = (bf16[1024,128]{1,0:T(8,128)(2,1)S(1)}, bf16[1024,128]{1,0:T(8,128)(2,1)}, u32[]{:S(2)}) copy-start(bf16[1024,128]{1,0:T(8,128)(2,1)} %param.18) | copy-start | bytes 786436
  7.2 225.6 %all-gather.3.cloned.1.call-start = ((), (), s32[]{:S(2)}) async-start(), calls=%async_computation.3 | async-start | bytes 2162688 | tf_op jit(solution)/shard_map/all_gather | solution.py:37
  16.3 15.5 %copy-start.4 = (bf16[192,1024]{1,0:T(8,128)(2,1)S(1)}, bf16[192,1024]{1,0:T(8,128)(2,1)}, u32[]{:S(2)}) copy-start(bf16[192,1024]{1,0:T(8,128)(2,1)} %param.21) | copy-start | bytes 1179652
  16.3 15.5 %copy-start.5 = (bf16[192,1024]{1,0:T(8,128)(2,1)S(1)}, bf16[192,1024]{1,0:T(8,128)(2,1)}, u32[]{:S(2)}) copy-start(bf16[192,1024]{1,0:T(8,128)(2,1)} %param.20) | copy-start | bytes 1179652
  17.9 13.9 %copy-start.6 = (bf16[192,1024]{1,0:T(8,128)(2,1)S(1)}, bf16[192,1024]{1,0:T(8,128)(2,1)}, u32[]{:S(2)}) copy-start(bf16[192,1024]{1,0:T(8,128)(2,1)} %param.19) | copy-start | bytes 1179652
  17.9 18.0 %copy-start.9 = (bf16[1,128,2,128]{3,2,1,0:T(2,128)(2,1)S(1)}, bf16[1,128,2,128]{3,2,1,0:T(2,128)(2,1)}, u32[]{:S(2)}) copy-start(bf16[1,128,2,128]{3,2,1,0:T(2,128)(2,1)} %param.15) | copy-start | bytes 196612
  17.9 41.9 %all-to-all-start = ((bf16[4,32,4,1024]{3,2,0,1:T(4,128)(2,1)}), bf16[4,32,4,1024]{3,2,0,1:T(4,128)(2,1)S(1)}, u32[]{:S(2)}, u32[]{:S(2)}) async-start(bf16[4,32,4,1024]{3,2,0,1:T(4,128)(2,1)} %copy.84), calls=%async_computation | async-start | bytes 2097152 | tf_op jit(solution)/shard_map/all_to_all | solution.py:121
  31.7 201.1 %all-gather.5.cloned.1.call-start = ((), (), s32[]{:S(2)}) async-start(), calls=%async_computation.4 | async-start | bytes 2162688 | tf_op jit(solution)/shard_map/all_gather | solution.py:38
  33.0 38.5 %collective-permute-start.15 = (bf16[3,192,1024]{2,1,0:T(8,128)(2,1)}, bf16[3,192,1024]{2,1,0:T(8,128)(2,1)}, u32[]{:S(2)}, u32[]{:S(2)}) collective-permute-start(bf16[3,192,1024]{2,1,0:T(8,128)(2,1)} %pad_maximum_fusion), channel_id=1, source_target_pairs={{0,1},{1,0},{2,3},{3,2},{4,5},{5,4},{6,7},{7,6},{8,9},{9,8},{10,11... | collective-permute-start | bytes 3538952 | tf_op jit(solution)/shard_map/ppermute | solution.py:9
  61.8 9.7 %copy-start.7 = (bf16[192,1024]{1,0:T(8,128)(2,1)S(1)}, bf16[192,1024]{1,0:T(8,128)(2,1)}, u32[]{:S(2)}) copy-start(bf16[192,1024]{1,0:T(8,128)(2,1)} %param.19) | copy-start | bytes 1179652
  63.2 20.5 %collective-permute-start = (bf16[1,16,4,1024]{3,2,1,0:T(4,128)(2,1)S(1)}, bf16[1,16,4,1024]{3,2,1,0:T(4,128)(2,1)S(1)}, u32[]{:S(2)}, u32[]{:S(2)}) collective-permute-start(bf16[1,16,4,1024]{3,2,1,0:T(4,128)(2,1)S(1)} %get-tuple-element.157), channel_id=1, source_target_pairs={{0,1},{1,0},{2,3},{3,2},{4,5},{5,4},{6,7},{7,6},{8,9},{9,8},{10,11... | collective-permute-start | bytes 393224 | tf_op jit(solution)/shard_map/ppermute | solution.py:149
  68.3 20.8 %collective-permute-start.1 = (bf16[1,16,4,1024]{3,2,1,0:T(4,128)(2,1)S(1)}, bf16[1,16,4,1024]{3,2,1,0:T(4,128)(2,1)S(1)}, u32[]{:S(2)}, u32[]{:S(2)}) collective-permute-start(bf16[1,16,4,1024]{3,2,1,0:T(4,128)(2,1)S(1)} %get-tuple-element.156), channel_id=1, source_target_pairs={{0,2},{1,3},{2,0},{3,1},{4,6},{5,7},{6,4},{7,5},{8,10},{9,11},{10,... | collective-permute-start | bytes 393224 | tf_op jit(solution)/shard_map/ppermute | solution.py:149
  74.9 16.3 %collective-permute-start.2 = (bf16[1,16,4,1024]{3,2,1,0:T(4,128)(2,1)S(1)}, bf16[1,16,4,1024]{3,2,1,0:T(4,128)(2,1)S(1)}, u32[]{:S(2)}, u32[]{:S(2)}) collective-permute-start(bf16[1,16,4,1024]{3,2,1,0:T(4,128)(2,1)S(1)} %get-tuple-element.155), channel_id=1, source_target_pairs={{0,3},{1,2},{2,1},{3,0},{4,7},{5,6},{6,5},{7,4},{8,11},{9,10},{10,... | collective-permute-start | bytes 393224 | tf_op jit(solution)/shard_map/ppermute | solution.py:149
  77.1 21.6 %collective-permute-start.3 = (bf16[1,16,4,1024]{3,2,1,0:T(4,128)(2,1)S(1)}, bf16[1,16,4,1024]{3,2,1,0:T(4,128)(2,1)S(1)}, u32[]{:S(2)}, u32[]{:S(2)}) collective-permute-start(bf16[1,16,4,1024]{3,2,1,0:T(4,128)(2,1)S(1)} %get-tuple-element.154), channel_id=1, source_target_pairs={{0,4},{1,5},{2,6},{3,7},{4,0},{5,1},{6,2},{7,3},{8,12},{9,13},{10,... | collective-permute-start | bytes 393224 | tf_op jit(solution)/shard_map/ppermute | solution.py:149
  81.3 23.5 %collective-permute-start.4 = (bf16[1,16,4,1024]{3,2,1,0:T(4,128)(2,1)S(1)}, bf16[1,16,4,1024]{3,2,1,0:T(4,128)(2,1)S(1)}, u32[]{:S(2)}, u32[]{:S(2)}) collective-permute-start(bf16[1,16,4,1024]{3,2,1,0:T(4,128)(2,1)S(1)} %get-tuple-element.153), channel_id=1, source_target_pairs={{0,5},{1,4},{2,7},{3,6},{4,1},{5,0},{6,3},{7,2},{8,13},{9,12},{10,... | collective-permute-start | bytes 393224 | tf_op jit(solution)/shard_map/ppermute | solution.py:149
  83.7 23.2 %collective-permute-start.5 = (bf16[1,16,4,1024]{3,2,1,0:T(4,128)(2,1)S(1)}, bf16[1,16,4,1024]{3,2,1,0:T(4,128)(2,1)S(1)}, u32[]{:S(2)}, u32[]{:S(2)}) collective-permute-start(bf16[1,16,4,1024]{3,2,1,0:T(4,128)(2,1)S(1)} %get-tuple-element.152), channel_id=1, source_target_pairs={{0,6},{1,7},{2,4},{3,5},{4,2},{5,3},{6,0},{7,1},{8,14},{9,15},{10,... | collective-permute-start | bytes 393224 | tf_op jit(solution)/shard_map/ppermute | solution.py:149
  89.1 34.5 %collective-permute-start.6 = (bf16[1,16,4,1024]{3,2,1,0:T(4,128)(2,1)S(1)}, bf16[1,16,4,1024]{3,2,1,0:T(4,128)(2,1)S(1)}, u32[]{:S(2)}, u32[]{:S(2)}) collective-permute-start(bf16[1,16,4,1024]{3,2,1,0:T(4,128)(2,1)S(1)} %get-tuple-element.151), channel_id=1, source_target_pairs={{0,7},{1,6},{2,5},{3,4},{4,3},{5,2},{6,1},{7,0},{8,15},{9,14},{10,... | collective-permute-start | bytes 393224 | tf_op jit(solution)/shard_map/ppermute | solution.py:149
  91.2 36.4 %collective-permute-start.7 = (bf16[1,16,4,1024]{3,2,1,0:T(4,128)(2,1)S(1)}, bf16[1,16,4,1024]{3,2,1,0:T(4,128)(2,1)S(1)}, u32[]{:S(2)}, u32[]{:S(2)}) collective-permute-start(bf16[1,16,4,1024]{3,2,1,0:T(4,128)(2,1)S(1)} %get-tuple-element.150), channel_id=1, source_target_pairs={{0,8},{1,9},{2,10},{3,11},{4,12},{5,13},{6,14},{7,15},{8,0},{9,1},... | collective-permute-start | bytes 393224 | tf_op jit(solution)/shard_map/ppermute | solution.py:149
  98.7 32.2 %collective-permute-start.8 = (bf16[1,16,4,1024]{3,2,1,0:T(4,128)(2,1)S(1)}, bf16[1,16,4,1024]{3,2,1,0:T(4,128)(2,1)S(1)}, u32[]{:S(2)}, u32[]{:S(2)}) collective-permute-start(bf16[1,16,4,1024]{3,2,1,0:T(4,128)(2,1)S(1)} %get-tuple-element.149), channel_id=1, source_target_pairs={{0,9},{1,8},{2,11},{3,10},{4,13},{5,12},{6,15},{7,14},{8,1},{9,0},... | collective-permute-start | bytes 393224 | tf_op jit(solution)/shard_map/ppermute | solution.py:149
  104.9 28.0 %collective-permute-start.9 = (bf16[1,16,4,1024]{3,2,1,0:T(4,128)(2,1)S(1)}, bf16[1,16,4,1024]{3,2,1,0:T(4,128)(2,1)S(1)}, u32[]{:S(2)}, u32[]{:S(2)}) collective-permute-start(bf16[1,16,4,1024]{3,2,1,0:T(4,128)(2,1)S(1)} %get-tuple-element.148), channel_id=1, source_target_pairs={{0,10},{1,11},{2,8},{3,9},{4,14},{5,15},{6,12},{7,13},{8,2},{9,3},... | collective-permute-start | bytes 393224 | tf_op jit(solution)/shard_map/ppermute | solution.py:149
  106.9 31.7 %collective-permute-start.10 = (bf16[1,16,4,1024]{3,2,1,0:T(4,128)(2,1)S(1)}, bf16[1,16,4,1024]{3,2,1,0:T(4,128)(2,1)S(1)}, u32[]{:S(2)}, u32[]{:S(2)}) collective-permute-start(bf16[1,16,4,1024]{3,2,1,0:T(4,128)(2,1)S(1)} %get-tuple-element.147), channel_id=1, source_target_pairs={{0,11},{1,10},{2,9},{3,8},{4,15},{5,14},{6,13},{7,12},{8,3},{9,2},... | collective-permute-start | bytes 393224 | tf_op jit(solution)/shard_map/ppermute | solution.py:149
  123.6 15.0 %collective-permute-start.11 = (bf16[1,16,4,1024]{3,2,1,0:T(4,128)(2,1)S(1)}, bf16[1,16,4,1024]{3,2,1,0:T(4,128)(2,1)S(1)}, u32[]{:S(2)}, u32[]{:S(2)}) collective-permute-start(bf16[1,16,4,1024]{3,2,1,0:T(4,128)(2,1)S(1)} %get-tuple-element.146), channel_id=1, source_target_pairs={{0,12},{1,13},{2,14},{3,15},{4,8},{5,9},{6,10},{7,11},{8,4},{9,5},... | collective-permute-start | bytes 393224 | tf_op jit(solution)/shard_map/ppermute | solution.py:149
  127.6 16.7 %collective-permute-start.12 = (bf16[1,16,4,1024]{3,2,1,0:T(4,128)(2,1)S(1)}, bf16[1,16,4,1024]{3,2,1,0:T(4,128)(2,1)S(1)}, u32[]{:S(2)}, u32[]{:S(2)}) collective-permute-start(bf16[1,16,4,1024]{3,2,1,0:T(4,128)(2,1)S(1)} %get-tuple-element.145), channel_id=1, source_target_pairs={{0,13},{1,12},{2,15},{3,14},{4,9},{5,8},{6,11},{7,10},{8,5},{9,4},... | collective-permute-start | bytes 393224 | tf_op jit(solution)/shard_map/ppermute | solution.py:149
  130.9 17.2 %collective-permute-start.13 = (bf16[1,16,4,1024]{3,2,1,0:T(4,128)(2,1)S(1)}, bf16[1,16,4,1024]{3,2,1,0:T(4,128)(2,1)S(1)}, u32[]{:S(2)}, u32[]{:S(2)}) collective-permute-start(bf16[1,16,4,1024]{3,2,1,0:T(4,128)(2,1)S(1)} %get-tuple-element.144), channel_id=1, source_target_pairs={{0,14},{1,15},{2,12},{3,13},{4,10},{5,11},{6,8},{7,9},{8,6},{9,7},... | collective-permute-start | bytes 393224 | tf_op jit(solution)/shard_map/ppermute | solution.py:149
  132.9 18.5 %collective-permute-start.14 = (bf16[1,16,4,1024]{3,2,1,0:T(4,128)(2,1)S(1)}, bf16[1,16,4,1024]{3,2,1,0:T(4,128)(2,1)S(1)}, u32[]{:S(2)}, u32[]{:S(2)}) collective-permute-start(bf16[1,16,4,1024]{3,2,1,0:T(4,128)(2,1)S(1)} %get-tuple-element.143), channel_id=1, source_target_pairs={{0,15},{1,14},{2,13},{3,12},{4,11},{5,10},{6,9},{7,8},{8,7},{9,6},... | collective-permute-start | bytes 393224 | tf_op jit(solution)/shard_map/ppermute | solution.py:149
  165.2 8.8 %copy-start.10 = (s32[1,128,2]{1,2,0:T(2,128)S(1)}, s32[1,128,2]{1,2,0:T(2,128)}, u32[]{:S(2)}) copy-start(s32[1,128,2]{1,2,0:T(2,128)} %param.16) | copy-start | bytes 3076
  165.3 57.6 %all-to-all-start.1 = ((bf16[16,16,4,1024]{3,1,2,0:T(8,128)(2,1)}), bf16[16,16,4,1024]{3,1,2,0:T(8,128)(2,1)S(1)}, u32[]{:S(2)}, u32[]{:S(2)}) async-start(bf16[16,16,4,1024]{3,1,2,0:T(8,128)(2,1)} %convolution_convert_fusion), calls=%async_computation.1 | async-start | bytes 4194304 | tf_op jit(solution)/shard_map/all_to_all | solution.py:155
  225.9 7.0 %copy-start.8 = (f32[2,8,128,128]{3,2,1,0:T(8,128)S(1)}, f32[2,8,128,128]{3,2,1,0:T(8,128)}, u32[]{:S(2)}) copy-start(f32[2,8,128,128]{3,2,1,0:T(8,128)} %custom-call.4) | copy-start | bytes 3145732
  227.7 96.6 %all-to-all-start.2 = ((bf16[4,32,4,1024]{3,2,0,1:T(4,128)(2,1)}), bf16[4,32,4,1024]{3,2,0,1:T(4,128)(2,1)S(1)}, u32[]{:S(2)}, u32[]{:S(2)}) async-start(bf16[4,32,4,1024]{3,2,0,1:T(4,128)(2,1)} %copy.88), calls=%async_computation.2 | async-start | bytes 2097152 | tf_op jit(solution)/shard_map/all_to_all | solution.py:162
  238.0 3.4 %copy-start.1 = (f32[2,512,128,8]{2,1,3,0:T(8,128)S(1)}, f32[2,512,128,8]{2,1,3,0:T(8,128)}, u32[]{:S(2)}) copy-start(f32[2,512,128,8]{2,1,3,0:T(8,128)} %get-tuple-element.219) | copy-start | bytes 12582916 | tf_op jit(solution)/shard_map/while
  271.7 3.4 %copy-start.1 = (f32[2,512,128,8]{2,1,3,0:T(8,128)S(1)}, f32[2,512,128,8]{2,1,3,0:T(8,128)}, u32[]{:S(2)}) copy-start(f32[2,512,128,8]{2,1,3,0:T(8,128)} %get-tuple-element.219) | copy-start | bytes 12582916 | tf_op jit(solution)/shard_map/while
  316.6 3.4 %copy-start.1 = (f32[2,512,128,8]{2,1,3,0:T(8,128)S(1)}, f32[2,512,128,8]{2,1,3,0:T(8,128)}, u32[]{:S(2)}) copy-start(f32[2,512,128,8]{2,1,3,0:T(8,128)} %get-tuple-element.219) | copy-start | bytes 12582916 | tf_op jit(solution)/shard_map/while
  (7 other events, 23.6 us)
Sparse Core Ops, SparseCore 0:
  11.8 87.4 all-gather.2
  103.0 80.6 all-gather.4
